TPU v7x, 256 devices: a whole 4x4x8 slice. The times are simulated.
256 devices in a mesh: dp: 8 (over z), seq: 32 (over y, x, core).
Axes of the slice: x: 4, y: 4, z: 8, core: 2. Of those that a mesh axis runs over, the one named last changes fastest.
Arguments:
- inputs: bfloat16 [8, 4096, 2048], P('dp', 'seq'), may hold values from -6 to 6
- weight_codes: bfloat16 [2048, 1280], P('seq'), may hold values from -4 to 4
- scales: bfloat16 [2048, 10], P('seq'), may hold values from 0.010986328 to 0.043945312
- log_decay: float32 [8, 16, 4096], P('dp', None, 'seq'), may hold values from -0.85 to 0, as said below
- cotangent: bfloat16 [8, 4096, 1024], P('dp', 'seq'), may hold values from -6 to 6
Outputs:
- grad_inputs: float32 [8, 4096, 2048], P('dp', 'seq')
- grad_weight: float32 [2048, 1280], P('seq')
Inputs may be any that keep to these rules, and one draw needn't show every extreme that they name: log_decay is negative everywhere.
All inputs are finite; a program needn't handle non-finite values.
Results may differ from a plain program's by a relative error of at most 0.017.
Values may be sent and summed in bfloat16 or wider, within the bound.
No kernel may reach another device: no remote copies, remote signals or barrier semaphores. Data moves between devices by JAX's collectives and lax.ppermute only.
A program may use at most 128 MiB of HBM per device.

v0:
```python
import math
import jax
import jax.numpy as jnp
from jax import lax
from jax.sharding import PartitionSpec as P


def shifted(value, axis, step, reverse):
    count = lax.axis_size(axis)
    if reverse:
        pairs = [(place, place - step) for place in range(step, count)]
    else:
        pairs = [(place, place + step) for place in range(count - step)]
    return lax.ppermute(value, axis, pairs)


def scan_entering(decay, state, axis, reverse):
    head_count = state.shape[0]
    packed = jnp.concatenate(
        [state.reshape(head_count, -1), jnp.broadcast_to(decay[:, None], (head_count, 128))], axis=1
    )
    split = packed.shape[1] - 128
    packed = shifted(packed, axis, 1, reverse)
    step = 1
    while step < lax.axis_size(axis):
        earlier = shifted(packed, axis, step, reverse)
        later_decay = packed[:, split:]
        packed = jnp.concatenate(
            [
                later_decay[:, :1] * earlier[:, :split] + packed[:, :split],
                earlier[:, split:] * later_decay,
            ],
            axis=1,
        )
        step *= 2
    return packed[:, :split].reshape(state.shape)


def dequantize(code_rows, scale_rows):
    row_count, col_count = code_rows.shape
    group_count = scale_rows.shape[1]
    spread = code_rows.astype(jnp.float32).reshape(row_count, group_count, col_count // group_count)
    spread = spread * scale_rows.astype(jnp.float32)[:, :, None]
    return spread.reshape(row_count, col_count).astype(jnp.bfloat16)


def block_prep(ld_block):
    cum_log = jnp.cumsum(ld_block, axis=1)
    input_scale = jnp.sqrt(-jnp.expm1(2.0 * ld_block))
    tail_weight = jnp.exp(cum_log[:, -1:] - cum_log) * input_scale
    return (cum_log, input_scale, tail_weight)


def weighted_pair(x_vals, grad_out, tail_weight, cum_log, inv_root):
    head_weight = jnp.exp(cum_log) * inv_root
    weighted_x = (x_vals.astype(jnp.float32) * tail_weight.T[:, :, None]).astype(jnp.bfloat16)
    weighted_g = (grad_out.astype(jnp.float32) * head_weight.T[:, :, None]).astype(jnp.bfloat16)
    return (weighted_x, weighted_g)


def summaries(x_vals, b_mat, c_mat, grad_out, ld_block):
    cum_log, input_scale, tail_weight = block_prep(ld_block)
    inv_root = 1.0 / math.sqrt(b_mat.shape[1])
    weighted_x, weighted_g = weighted_pair(x_vals, grad_out, tail_weight, cum_log, inv_root)
    fwd_state = jnp.einsum("sn,shp->hnp", b_mat, weighted_x, preferred_element_type=jnp.float32)
    back_state = jnp.einsum("tn,thp->hnp", c_mat, weighted_g, preferred_element_type=jnp.float32)
    return (jnp.exp(cum_log[:, -1]), fwd_state, back_state)


def block_grads(x_vals, b_mat, c_mat, grad_out, ld_block, state_in, back_in):
    block_len = ld_block.shape[1]
    cum_log, input_scale, tail_weight = block_prep(ld_block)
    inv_root = 1.0 / math.sqrt(b_mat.shape[1])
    weighted_x, weighted_g = weighted_pair(x_vals, grad_out, tail_weight, cum_log, inv_root)
    row_ids = lax.broadcasted_iota(jnp.int32, (block_len, block_len), 0)
    col_ids = lax.broadcasted_iota(jnp.int32, (block_len, block_len), 1)
    lower_mask = (row_ids >= col_ids)[None]
    log_gap = cum_log[:, :, None] - cum_log[:, None, :]
    decay_mat = jnp.where(lower_mask, jnp.exp(jnp.where(lower_mask, log_gap, 0.0)), 0.0)
    state_low = state_in.astype(jnp.bfloat16)
    back_low = back_in.astype(jnp.bfloat16)
    x_dot_g = jnp.einsum("thp,shp->hts", grad_out, x_vals, preferred_element_type=jnp.float32)
    c_dot_b = jnp.dot(c_mat, b_mat.T, preferred_element_type=jnp.float32)
    mix_weights = (
        jnp.sum(decay_mat * input_scale[:, None, :] * x_dot_g, axis=0) * inv_root
    ).astype(jnp.bfloat16)
    d_c = jnp.einsum("hnp,thp->tn", state_low, weighted_g, preferred_element_type=jnp.float32)
    d_c = d_c + jnp.dot(mix_weights, b_mat, preferred_element_type=jnp.float32)
    d_b = jnp.einsum("hnp,thp->tn", back_low, weighted_x, preferred_element_type=jnp.float32)
    d_b = d_b + jnp.dot(mix_weights.T, c_mat, preferred_element_type=jnp.float32)
    d_x = (
        jnp.einsum("tn,hnp->thp", b_mat, back_low, preferred_element_type=jnp.float32)
        * tail_weight.T[:, :, None]
    )
    inner_weights = (decay_mat * c_dot_b[None] * inv_root).astype(jnp.bfloat16)
    inner = jnp.einsum("hus,uhp->shp", inner_weights, grad_out, preferred_element_type=jnp.float32)
    d_x = d_x + input_scale.T[:, :, None] * inner
    return (d_x, d_b, d_c)


def state_chain(decays, adds, start, backward):

    def step(carry, item):
        return (item[0][:, None, None] * carry + item[1], carry)

    return lax.scan(step, start, (decays, adds), reverse=backward)


def local(inputs, weight_codes, scales, log_decay, cotangent):
    tok_count = inputs.shape[1]
    features = inputs[0]
    grad_out = cotangent[0]
    head_count = log_decay.shape[1]
    hp_width = grad_out.shape[1]
    head_dim = hp_width // head_count
    proj_width = weight_codes.shape[1]
    state_width = (proj_width - hp_width) // 2
    weights = lax.all_gather(dequantize(weight_codes, scales), "seq", axis=0, tiled=True)
    projected = jnp.dot(features, weights, preferred_element_type=jnp.float32).astype(jnp.bfloat16)
    block_len = min(128, tok_count)
    block_count = tok_count // block_len
    x_blocks = projected[:, :hp_width].reshape(block_count, block_len, head_count, head_dim)
    b_blocks = projected[:, hp_width : hp_width + state_width].reshape(
        block_count, block_len, state_width
    )
    c_blocks = projected[:, hp_width + state_width :].reshape(block_count, block_len, state_width)
    g_blocks = grad_out.reshape(block_count, block_len, head_count, head_dim)
    ld_blocks = log_decay[0].reshape(head_count, block_count, block_len).transpose(1, 0, 2)
    decays, fwd_states, back_states = jax.vmap(summaries)(
        x_blocks, b_blocks, c_blocks, g_blocks, ld_blocks
    )
    zero_state = jnp.zeros((head_count, state_width, head_dim), jnp.float32)
    dev_decay = jnp.prod(decays, axis=0)
    dev_fwd, unused_a = state_chain(decays, fwd_states, zero_state, False)
    dev_back, unused_b = state_chain(decays, back_states, zero_state, True)
    carried = (None, scan_entering(dev_decay, dev_fwd, "seq", False))
    returned = (None, scan_entering(dev_decay, dev_back, "seq", True))
    unused_c, state_starts = state_chain(decays, fwd_states, carried[1], False)
    unused_d, back_starts = state_chain(decays, back_states, returned[1], True)
    d_x, d_b, d_c = lax.map(
        lambda block_item: block_grads(*block_item),
        (x_blocks, b_blocks, c_blocks, g_blocks, ld_blocks, state_starts, back_starts),
    )
    d_proj = jnp.concatenate(
        [
            d_x.reshape(tok_count, hp_width),
            d_b.reshape(tok_count, state_width),
            d_c.reshape(tok_count, state_width),
        ],
        axis=1,
    ).astype(jnp.bfloat16)
    grad_in = lax.dot_general(
        d_proj, weights, (((1,), (1,)), ((), ())), preferred_element_type=jnp.float32
    )
    seq_count = lax.axis_size("seq")
    group_count = lax.axis_size("dp")
    norm_factor = 1.0 / math.sqrt(group_count * seq_count * tok_count)
    partial_grad = lax.psum_scatter(
        lax.dot_general(
            features, d_proj, (((0,), (0,)), ((), ())), preferred_element_type=jnp.float32
        ),
        "seq",
        scatter_dimension=0,
        tiled=True,
    )
    summed_grad = lax.psum(partial_grad, "dp")
    return (grad_in[None], summed_grad * norm_factor)


def solution(mesh):
    placed = (
        P("dp", "seq", None),
        P("seq", None),
        P("seq", None),
        P("dp", None, "seq"),
        P("dp", "seq", None),
    )
    return jax.shard_map(
        local,
        mesh=mesh,
        in_specs=placed,
        out_specs=(P("dp", "seq", None), P("seq", None)),
        check_vma=False,
    )
```

profile of v0, /device:TPU:2, one launch (start us, length us, event | category | flops | bytes accessed | tf_op | source)
XLA Modules:
  0.0 389.5 jit_solution(13289274053930057519)
XLA Ops:
  7.2 0.8 copy.49
  8.1 0.2 mul.339
  8.2 1.7 fusion.30
  10.0 1.0 reduce_window_sum.23
  11.0 1.0 reduce_window_sum.24
  12.0 1.1 copy.50
  13.1 0.2 slice_reduce_fusion.5
  13.3 0.2 slice_reduce_fusion.11
  13.5 0.8 multiply_bitcast_fusion.3
  14.2 1.3 fusion.48
  15.7 50.6 %all-gather.2.cloned.1.call-done = bf16[2048,1280]{1,0:T(8,128)(2,1)} async-done(((bf16[64,1280]{1,0:T(8,128)(2,1)}), bf16[2048,1280]{1,0:T(8,128)(2,1)}) %all-gather.2.cloned.1.call-update) | async-done | bytes 5242896 | tf_op jit(solution)/shard_map/all_gather | solution.py:118
  66.2 4.1 %fusion = bf16[128,1280]{0,1:T(8,128)(2,1)S(1)} fusion(bf16[2048,1280]{1,0:T(8,128)(2,1)} %all-gather.2.cloned.1.call-done, bf16[1,128,2048]{2,1,0:T(8,128)(2,1)S(1)} %copy-done), kind=kOutput, calls=%fused_computation.3 | convolution fusion | flops 671252480 | bytes 6094848 | tf_op jit(solution)/shard_map/dot_general | solution.py:119
  70.3 0.2 convolution_bitcast_fusion.5
  70.5 0.8 fusion.10
  71.3 0.2 convolution_bitcast_fusion.3
  71.5 0.3 copy.60
  71.9 0.4 squeeze.57
  72.3 0.3 copy.52
  72.6 0.4 squeeze.53
  73.2 2.7 collective-permute-start
  75.9 1.9 collective-permute-start.6
  77.9 4.8 %collective-permute-done = f32[16,8320]{1,0:T(8,128)S(1)} collective-permute-done((f32[16,8320]{1,0:T(8,128)S(1)}, f32[16,8320]{1,0:T(8,128)S(1)}, u32[]{:S(2)}, u32[]{:S(2)}) %collective-permute-start) | collective-permute-done | bytes 532512 | tf_op jit(solution)/shard_map/ppermute | solution.py:14
  82.7 3.8 collective-permute-start.1
  86.5 0.9 fusion.2
  87.4 0.8 fusion.34
  88.3 1.9 collective-permute-start.7
  90.4 2.8 collective-permute-done.1
  93.4 1.9 collective-permute-start.2
  95.4 3.5 collective-permute-done.7
  99.0 3.3 collective-permute-start.8
  102.6 6.7 %collective-permute-done.2 = f32[16,8320]{1,0:T(8,128)S(1)} collective-permute-done((f32[16,8320]{1,0:T(8,128)S(1)}, f32[16,8320]{1,0:T(8,128)S(1)}, u32[]{:S(2)}, u32[]{:S(2)}) %collective-permute-start.2) | collective-permute-done | bytes 532512 | tf_op jit(solution)/shard_map/ppermute | solution.py:14
  109.3 0.1 fusion.21
  109.5 1.3 collective-permute-start.3
  110.8 3.1 collective-permute-done.8
  114.1 19.8 %collective-permute-start.9 = (f32[16,8320]{1,0:T(8,128)S(1)}, f32[16,8320]{1,0:T(8,128)S(1)}, u32[]{:S(2)}, u32[]{:S(2)}) collective-permute-start(f32[16,8320]{1,0:T(8,128)S(1)} %pad_maximum_fusion.7), channel_id=1, source_target_pairs={{0,4},{1,5},{2,6},{3,7},{4,8},{5,9},{6,10},{7,11},{8,12},{9,13},{1... | collective-permute-start | bytes 1597448 | tf_op jit(solution)/shard_map/ppermute | solution.py:14
  134.2 0.1 fusion.20
  134.4 1.3 collective-permute-start.4
  135.7 7.2 %collective-permute-done.9 = f32[16,8320]{1,0:T(8,128)S(1)} collective-permute-done((f32[16,8320]{1,0:T(8,128)S(1)}, f32[16,8320]{1,0:T(8,128)S(1)}, u32[]{:S(2)}, u32[]{:S(2)}) %collective-permute-start.9) | collective-permute-done | bytes 532512 | tf_op jit(solution)/shard_map/ppermute | solution.py:14
  143.1 5.6 %collective-permute-start.10 = (f32[16,8320]{1,0:T(8,128)S(1)}, f32[16,8320]{1,0:T(8,128)S(1)}, u32[]{:S(2)}, u32[]{:S(2)}) collective-permute-start(f32[16,8320]{1,0:T(8,128)S(1)} %pad_maximum_fusion.8), channel_id=1, source_target_pairs={{0,8},{1,9},{2,10},{3,11},{4,12},{5,13},{6,14},{7,15},{8,16},{9,17... | collective-permute-start | bytes 1597448 | tf_op jit(solution)/shard_map/ppermute | solution.py:14
  149.0 0.5 collective-permute-done.4
  149.6 1.3 collective-permute-start.5
  150.9 4.6 %collective-permute-done.10 = f32[16,8320]{1,0:T(8,128)S(1)} collective-permute-done((f32[16,8320]{1,0:T(8,128)S(1)}, f32[16,8320]{1,0:T(8,128)S(1)}, u32[]{:S(2)}, u32[]{:S(2)}) %collective-permute-start.10) | collective-permute-done | bytes 532512 | tf_op jit(solution)/shard_map/ppermute | solution.py:14
  155.7 10.0 %collective-permute-start.11 = (f32[16,8320]{1,0:T(8,128)S(1)}, f32[16,8320]{1,0:T(8,128)}, u32[]{:S(2)}, u32[]{:S(2)}) collective-permute-start(f32[16,8320]{1,0:T(8,128)S(1)} %pad_maximum_fusion.9), channel_id=1, source_target_pairs={{0,16},{1,17},{2,18},{3,19},{4,20},{5,21},{6,22},{7,23},{8,24},{9,... | collective-permute-start | bytes 1597448 | tf_op jit(solution)/shard_map/ppermute | solution.py:14
  165.8 0.6 slice_reduce_fusion.1
  166.4 2.6 collective-permute-done.5
  169.0 0.2 fusion.18
  169.1 0.5 convert_element_type.100
  169.7 0.2 copy.54
  169.9 0.9 convolution_bitcast_fusion.7
  170.8 0.2 fusion.37
  171.0 0.6 collective-permute-done.11
  171.7 1.2 fusion.13
  172.8 0.5 convert_element_type.111
  173.4 1.0 fusion.6
  174.4 0.3 convolution_bitcast_fusion.6
  174.8 1.4 fusion.5
  176.3 5.3 %convolution_bitcast_fusion = f32[2048,1280]{0,1:T(8,128)} fusion(bf16[1,128,2048]{2,1,0:T(8,128)(2,1)S(1)} %copy-done, bf16[128,128]{0,1:T(8,128)(2,1)S(1)} %fusion.7, bf16[128,128]{0,1:T(8,128)(2,1)S(1)} %fusion.6, bf16[128,1024]{0,1:T(8,128)(2,1)S(1)} %bitcast.105), kind=kOutput, calls=%fused_computation | convolution fusion | flops 672071680 | bytes 11337728 | tf_op jit(solution)/shard_map/dot_general | solution.py:159
  181.6 11.3 %copy.72 = f32[2048,1280]{1,0:T(8,128)} copy(f32[2048,1280]{0,1:T(8,128)} %convolution_bitcast_fusion) | data formatting | bytes 20971520
  193.0 111.7 %reduce-scatter.4.cloned.1.call-done = f32[64,1280]{1,0:T(8,128)} async-done(((f32[2048,1280]{1,0:T(8,128)}), f32[64,1280]{1,0:T(8,128)}) %reduce-scatter.4.cloned.1.call-update) | async-done | bytes 327696
  304.7 2.0 copy.73
  306.8 5.3 %convolution_bitcast_fusion.1 = f32[1,128,2048]{2,1,0:T(8,128)} fusion(bf16[2048,1280]{1,0:T(8,128)(2,1)} %all-gather.2.cloned.1.call-done, bf16[128,128]{0,1:T(8,128)(2,1)S(1)} %fusion.7, bf16[128,128]{0,1:T(8,128)(2,1)S(1)} %fusion.6, bf16[128,1024]{0,1:T(8,128)(2,1)S(1)} %bitcast.106), kind=kOutput, calls=%fused_computation.1 | convolution fusion | flops 672071680 | bytes 6619136 | tf_op jit(solution)/shard_map/dot_general | solution.py:152
  312.1 68.8 %all-reduce.2.cloned.1.call-done = f32[64,1280]{0,1:T(8,128)} async-done(((f32[64,1280]{0,1:T(8,128)}), f32[64,1280]{0,1:T(8,128)}) %all-reduce.2.cloned.1.call-update) | async-done | bytes 327696 | tf_op jit(solution)/shard_map/psum | solution.py:166
  380.9 1.1 broadcast_multiply_fusion
  382.1 0.9 copy.62
  (55 shorter events, 2.8 us)
Async XLA Ops:
  7.2 59.1 %copy-start = (bf16[1,128,2048]{2,1,0:T(8,128)(2,1)S(1)}, bf16[1,128,2048]{2,1,0:T(8,128)(2,1)}, u32[]{:S(2)}) copy-start(bf16[1,128,2048]{2,1,0:T(8,128)(2,1)} %param.5) | copy-start | bytes 1572868
  7.2 59.0 %all-gather.2.cloned.1.call-start = ((), (), s32[]{:S(2)}) async-start(), calls=%async_computation.1 | async-start | bytes 5406720 | tf_op jit(solution)/shard_map/all_gather | solution.py:118
  10.0 294.7 %reduce-scatter.4.cloned.1.call-start = ((), (), s32[]{:S(2)}) async-start(), calls=%async_computation.3 | async-start | bytes 10813440
  15.6 55.8 %copy-start.2 = (f32[128,16]{0,1:T(8,128)}, f32[128,16]{0,1:T(8,128)S(1)}, u32[]{:S(2)}) copy-start(f32[128,16]{0,1:T(8,128)S(1)} %get-tuple-element.80) | copy-start | bytes 24580
  73.2 9.4 %collective-permute-start = (f32[16,8320]{1,0:T(8,128)S(1)}, f32[16,8320]{1,0:T(8,128)S(1)}, u32[]{:S(2)}, u32[]{:S(2)}) collective-permute-start(f32[16,8320]{1,0:T(8,128)S(1)} %get-tuple-element.94), channel_id=1, source_target_pairs={{1,0},{2,1},{3,2},{4,3},{5,4},{6,5},{7,6},{8,7},{9,8},{10,9},{11,1... | collective-permute-start | bytes 1597448 | tf_op jit(solution)/shard_map/ppermute | solution.py:14
  75.9 12.4 %collective-permute-start.6 = (f32[16,8320]{1,0:T(8,128)S(1)}, f32[16,8320]{1,0:T(8,128)S(1)}, u32[]{:S(2)}, u32[]{:S(2)}) collective-permute-start(f32[16,8320]{1,0:T(8,128)S(1)} %get-tuple-element.95), channel_id=1, source_target_pairs={{0,1},{1,2},{2,3},{3,4},{4,5},{5,6},{6,7},{7,8},{8,9},{9,10},{10,1... | collective-permute-start | bytes 1597448 | tf_op jit(solution)/shard_map/ppermute | solution.py:14
  77.9 31.6 %copy-start.3 = (pred[128,128]{0,1:T(8,128)(4,1)}, pred[128,128]{0,1:T(8,128)(4,1)S(1)}, u32[]{:S(2)}) copy-start(pred[128,128]{0,1:T(8,128)(4,1)S(1)} %iota_compare_fusion) | copy-start | bytes 49156
  82.7 10.6 %collective-permute-start.1 = (f32[16,8320]{1,0:T(8,128)S(1)}, f32[16,8320]{1,0:T(8,128)S(1)}, u32[]{:S(2)}, u32[]{:S(2)}) collective-permute-start(f32[16,8320]{1,0:T(8,128)S(1)} %collective-permute-done), channel_id=1, source_target_pairs={{1,0},{2,1},{3,2},{4,3},{5,4},{6,5},{7,6},{8,7},{9,8},{10,9},{11,1... | collective-permute-start | bytes 1597448 | tf_op jit(solution)/shard_map/ppermute | solution.py:14
  88.3 10.6 %collective-permute-start.7 = (f32[16,8320]{1,0:T(8,128)S(1)}, f32[16,8320]{1,0:T(8,128)S(1)}, u32[]{:S(2)}, u32[]{:S(2)}) collective-permute-start(f32[16,8320]{1,0:T(8,128)S(1)} %collective-permute-done.6), channel_id=1, source_target_pairs={{0,1},{1,2},{2,3},{3,4},{4,5},{5,6},{6,7},{7,8},{8,9},{9,10},{10,1... | collective-permute-start | bytes 1597448 | tf_op jit(solution)/shard_map/ppermute | solution.py:14
  93.4 15.9 %collective-permute-start.2 = (f32[16,8320]{1,0:T(8,128)S(1)}, f32[16,8320]{1,0:T(8,128)S(1)}, u32[]{:S(2)}, u32[]{:S(2)}) collective-permute-start(f32[16,8320]{1,0:T(8,128)S(1)} %pad_maximum_fusion.2), channel_id=1, source_target_pairs={{2,0},{3,1},{4,2},{5,3},{6,4},{7,5},{8,6},{9,7},{10,8},{11,9},{12,... | collective-permute-start | bytes 1597448 | tf_op jit(solution)/shard_map/ppermute | solution.py:14
  99.0 14.9 %collective-permute-start.8 = (f32[16,8320]{1,0:T(8,128)S(1)}, f32[16,8320]{1,0:T(8,128)S(1)}, u32[]{:S(2)}, u32[]{:S(2)}) collective-permute-start(f32[16,8320]{1,0:T(8,128)S(1)} %pad_maximum_fusion.6), channel_id=1, source_target_pairs={{0,2},{1,3},{2,4},{3,5},{4,6},{5,7},{6,8},{7,9},{8,10},{9,11},{10,... | collective-permute-start | bytes 1597448 | tf_op jit(solution)/shard_map/ppermute | solution.py:14
  109.5 24.7 %collective-permute-start.3 = (f32[16,8320]{1,0:T(8,128)S(1)}, f32[16,8320]{1,0:T(8,128)S(1)}, u32[]{:S(2)}, u32[]{:S(2)}) collective-permute-start(f32[16,8320]{1,0:T(8,128)S(1)} %pad_maximum_fusion.3), channel_id=1, source_target_pairs={{4,0},{5,1},{6,2},{7,3},{8,4},{9,5},{10,6},{11,7},{12,8},{13,9},{1... | collective-permute-start | bytes 1597448 | tf_op jit(solution)/shard_map/ppermute | solution.py:14
  114.1 28.8 %collective-permute-start.9 = (f32[16,8320]{1,0:T(8,128)S(1)}, f32[16,8320]{1,0:T(8,128)S(1)}, u32[]{:S(2)}, u32[]{:S(2)}) collective-permute-start(f32[16,8320]{1,0:T(8,128)S(1)} %pad_maximum_fusion.7), channel_id=1, source_target_pairs={{0,4},{1,5},{2,6},{3,7},{4,8},{5,9},{6,10},{7,11},{8,12},{9,13},{1... | collective-permute-start | bytes 1597448 | tf_op jit(solution)/shard_map/ppermute | solution.py:14
  134.4 15.0 %collective-permute-start.4 = (f32[16,8320]{1,0:T(8,128)S(1)}, f32[16,8320]{1,0:T(8,128)S(1)}, u32[]{:S(2)}, u32[]{:S(2)}) collective-permute-start(f32[16,8320]{1,0:T(8,128)S(1)} %pad_maximum_fusion.4), channel_id=1, source_target_pairs={{8,0},{9,1},{10,2},{11,3},{12,4},{13,5},{14,6},{15,7},{16,8},{17,9... | collective-permute-start | bytes 1597448 | tf_op jit(solution)/shard_map/ppermute | solution.py:14
  142.9 27.0 %copy-start.1 = (bf16[128,1024]{0,1:T(8,128)(2,1)S(1)}, bf16[128,1024]{0,1:T(8,128)(2,1)}, u32[]{:S(2)}) copy-start(bf16[128,1024]{0,1:T(8,128)(2,1)} %get-tuple-element.75) | copy-start | bytes 786436
  143.1 12.5 %collective-permute-start.10 = (f32[16,8320]{1,0:T(8,128)S(1)}, f32[16,8320]{1,0:T(8,128)S(1)}, u32[]{:S(2)}, u32[]{:S(2)}) collective-permute-start(f32[16,8320]{1,0:T(8,128)S(1)} %pad_maximum_fusion.8), channel_id=1, source_target_pairs={{0,8},{1,9},{2,10},{3,11},{4,12},{5,13},{6,14},{7,15},{8,16},{9,17... | collective-permute-start | bytes 1597448 | tf_op jit(solution)/shard_map/ppermute | solution.py:14
  149.6 19.3 %collective-permute-start.5 = (f32[16,8320]{1,0:T(8,128)S(1)}, f32[16,8320]{1,0:T(8,128)S(1)}, u32[]{:S(2)}, u32[]{:S(2)}) collective-permute-start(f32[16,8320]{1,0:T(8,128)S(1)} %pad_maximum_fusion.5), channel_id=1, source_target_pairs={{16,0},{17,1},{18,2},{19,3},{20,4},{21,5},{22,6},{23,7},{24,8},{25... | collective-permute-start | bytes 1597448 | tf_op jit(solution)/shard_map/ppermute | solution.py:14
  155.7 15.9 %collective-permute-start.11 = (f32[16,8320]{1,0:T(8,128)S(1)}, f32[16,8320]{1,0:T(8,128)}, u32[]{:S(2)}, u32[]{:S(2)}) collective-permute-start(f32[16,8320]{1,0:T(8,128)S(1)} %pad_maximum_fusion.9), channel_id=1, source_target_pairs={{0,16},{1,17},{2,18},{3,19},{4,20},{5,21},{6,22},{7,23},{8,24},{9,... | collective-permute-start | bytes 1597448 | tf_op jit(solution)/shard_map/ppermute | solution.py:14
  192.9 188.0 %all-reduce.2.cloned.1.call-start = ((), (), s32[]{:S(2)}) async-start(), calls=%async_computation.2 | async-start | bytes 1310720 | tf_op jit(solution)/shard_map/psum | solution.py:166
Sparse Core Ops, SparseCore 0:
  11.1 55.0 all-gather.1
  193.1 111.5 reduce-scatter.3
  307.2 73.7 all-reduce.1
where the time goes:
time: 391 us; the launch traced here: 390 us
  waiting for transfers between devices  268 us (69%)
  starting transfers between devices  55 us (14%)
  local copies, waits for them, and re-layouts  21.2 us (5%)
  matrix products  20.9 us (5%)
  between operations  14.1 us (4%)
  other arithmetic  10.7 us (3%)
    unnamed x4, waiting for transfers between devices  112 us
    psum x1, waiting for transfers between devices, local(): summed_grad = lax.psum(partial_grad, 'dp')  68.8 us
    ppermute x12, starting transfers between devices, shifted(): return lax.ppermute(value, axis, pairs)  54.8 us
    all_gather x1, waiting for transfers between devices, local(): lax.all_gather(dequantize(weight_codes, scales), 'seq', axis=0, tiled=True)  50.6 us
    ppermute x12, waiting for transfers between devices, shifted(): return lax.ppermute(value, axis, pairs)  36.5 us
    unnamed x12, local copies, waits for them, and re-layouts  15.4 us
  transfers between devices with their start and end apart: 15, of which 13 were waited for; matrix products, arithmetic and copies ran while one was open for 5% of the time, Pallas kernels for 0%

commit v1 on v0

--- a/solution.py
+++ b/solution.py
@@ -115,7 +115,12 @@
     head_dim = hp_width // head_count
     proj_width = weight_codes.shape[1]
     state_width = (proj_width - hp_width) // 2
-    weights = lax.all_gather(dequantize(weight_codes, scales), "seq", axis=0, tiled=True)
+    weights = jnp.concatenate(
+        lax.all_to_all(
+            jnp.stack([dequantize(weight_codes, scales)] * lax.axis_size("seq")), "seq", 0, 0
+        ),
+        axis=0,
+    )
     projected = jnp.dot(features, weights, preferred_element_type=jnp.float32).astype(jnp.bfloat16)
     block_len = min(128, tok_count)
     block_count = tok_count // block_len

time: 391 us -> 409 us (1.046)
  waiting for transfers between devices: 268 us -> 281 us
  starting transfers between devices: 55 us -> 61 us
    all_to_all x0 -> x1, waiting for transfers between devices: none -> 61.2 us  [local(): lax.all_to_all(jnp.stack([dequantize(weight_codes, scales)] * lax.axis_si...]
    all_gather x1 -> x0, waiting for transfers between devices: 50.6 us -> none  [local(): lax.all_gather(dequantize(weight_codes, scales), 'seq', axis=0, tiled=True)]
    all_to_all x0 -> x1, starting transfers between devices: none -> 7.8 us  [local(): lax.all_to_all(jnp.stack([dequantize(weight_codes, scales)] * lax.axis_si...]
    unnamed x4 -> x3, waiting for transfers between devices: 112 us -> 113 us
    unnamed x12 -> x16, local copies, waits for them, and re-layouts: 15.4 us -> 14.5 us
  transfers between devices with their start and end apart: 15 -> 15, of which waited for: 13 -> 13; matrix products, arithmetic and copies ran while one was open for 5% -> 3% of each run, Pallas kernels for 0% -> 0%
where the time goes in v1:
time: 409 us; the launch traced here: 408 us
  waiting for transfers between devices  281 us (69%)
  starting transfers between devices  61 us (15%)
  local copies, waits for them, and re-layouts  23.3 us (6%)
  matrix products  20.9 us (5%)
  between operations  14.5 us (4%)
  other arithmetic  7.21 us (2%)
    unnamed x3, waiting for transfers between devices  113 us
    psum x1, waiting for transfers between devices, local(): summed_grad = lax.psum(partial_grad, 'dp')  68.8 us
    all_to_all x1, waiting for transfers between devices, local(): lax.all_to_all(jnp.stack([dequantize(weight_codes, scales)] * lax.axis_si...  61.2 us
    ppermute x12, starting transfers between devices, shifted(): return lax.ppermute(value, axis, pairs)  53.1 us
    ppermute x12, waiting for transfers between devices, shifted(): return lax.ppermute(value, axis, pairs)  37.9 us
    unnamed x16, local copies, waits for them, and re-layouts  14.5 us
  transfers between devices with their start and end apart: 15, of which 13 were waited for; matrix products, arithmetic and copies ran while one was open for 3% of the time, Pallas kernels for 0%

profile of v1, /device:TPU:2, one launch (start us, length us, event | category | flops | bytes accessed | tf_op | source)
XLA Modules:
  0.0 407.9 jit_solution(5325029210819385870)
XLA Ops:
  7.2 0.8 copy.49
  8.0 0.2 mul.339
  8.2 1.0 fusion.30
  9.2 2.9 stack.2
  12.1 7.8 %all-to-all-start = ((bf16[32,64,1280]{2,1,0:T(8,128)(2,1)}), bf16[32,64,1280]{2,1,0:T(8,128)(2,1)}, u32[]{:S(2)}, u32[]{:S(2)}) async-start(bf16[32,64,1280]{2,1,0:T(8,128)(2,1)} %stack.2), calls=%async_computation | async-start | bytes 10485760 | tf_op jit(solution)/shard_map/all_to_all | solution.py:119
  20.0 0.3 reduce_window_sum.23
  20.3 0.3 reduce_window_sum.24
  20.6 0.2 copy.50
  20.8 0.2 slice_reduce_fusion.5
  20.9 0.2 slice_reduce_fusion.11
  21.2 0.6 fusion.48
  21.9 61.2 %all-to-all-done = bf16[32,64,1280]{2,1,0:T(8,128)(2,1)} async-done(((bf16[32,64,1280]{2,1,0:T(8,128)(2,1)}), bf16[32,64,1280]{2,1,0:T(8,128)(2,1)}, u32[]{:S(2)}, u32[]{:S(2)}) %all-to-all-start) | async-done | bytes 5242912 | tf_op jit(solution)/shard_map/all_to_all | solution.py:119
  83.1 4.1 fusion
  87.2 0.2 convolution_bitcast_fusion.5
  87.4 0.8 fusion.10
  88.2 0.2 convolution_bitcast_fusion.3
  88.4 0.3 copy.60
  88.8 0.4 squeeze.57
  89.1 0.3 copy.52
  89.5 0.4 squeeze.53
  90.1 1.9 collective-permute-start
  92.0 2.4 collective-permute-start.6
  94.5 4.3 %collective-permute-done = f32[16,8320]{1,0:T(8,128)S(1)} collective-permute-done((f32[16,8320]{1,0:T(8,128)S(1)}, f32[16,8320]{1,0:T(8,128)S(1)}, u32[]{:S(2)}, u32[]{:S(2)}) %collective-permute-start) | collective-permute-done | bytes 532512 | tf_op jit(solution)/shard_map/ppermute | solution.py:14
  98.8 3.8 collective-permute-start.1
  102.6 0.9 fusion.2
  103.6 0.8 fusion.34
  104.4 2.1 collective-permute-start.7
  106.7 2.7 collective-permute-done.1
  109.6 1.9 collective-permute-start.2
  111.5 3.5 collective-permute-done.7
  115.2 3.7 collective-permute-start.8
  119.1 5.9 %collective-permute-done.2 = f32[16,8320]{1,0:T(8,128)S(1)} collective-permute-done((f32[16,8320]{1,0:T(8,128)S(1)}, f32[16,8320]{1,0:T(8,128)S(1)}, u32[]{:S(2)}, u32[]{:S(2)}) %collective-permute-start.2) | collective-permute-done | bytes 532512 | tf_op jit(solution)/shard_map/ppermute | solution.py:14
  125.2 1.3 collective-permute-start.3
  126.5 4.0 collective-permute-done.8
  130.6 20.8 %collective-permute-start.9 = (f32[16,8320]{1,0:T(8,128)S(1)}, f32[16,8320]{1,0:T(8,128)S(1)}, u32[]{:S(2)}, u32[]{:S(2)}) collective-permute-start(f32[16,8320]{1,0:T(8,128)S(1)} %pad_maximum_fusion.7), channel_id=1, source_target_pairs={{0,4},{1,5},{2,6},{3,7},{4,8},{5,9},{6,10},{7,11},{8,12},{9,13},{1... | collective-permute-start | bytes 1597448 | tf_op jit(solution)/shard_map/ppermute | solution.py:14
  151.7 0.1 fusion.20
  151.9 1.3 collective-permute-start.4
  153.2 7.4 %collective-permute-done.9 = f32[16,8320]{1,0:T(8,128)S(1)} collective-permute-done((f32[16,8320]{1,0:T(8,128)S(1)}, f32[16,8320]{1,0:T(8,128)S(1)}, u32[]{:S(2)}, u32[]{:S(2)}) %collective-permute-start.9) | collective-permute-done | bytes 532512 | tf_op jit(solution)/shard_map/ppermute | solution.py:14
  160.7 4.4 %collective-permute-start.10 = (f32[16,8320]{1,0:T(8,128)S(1)}, f32[16,8320]{1,0:T(8,128)S(1)}, u32[]{:S(2)}, u32[]{:S(2)}) collective-permute-start(f32[16,8320]{1,0:T(8,128)S(1)} %pad_maximum_fusion.8), channel_id=1, source_target_pairs={{0,8},{1,9},{2,10},{3,11},{4,12},{5,13},{6,14},{7,15},{8,16},{9,17... | collective-permute-start | bytes 1597448 | tf_op jit(solution)/shard_map/ppermute | solution.py:14
  165.3 0.5 collective-permute-done.4
  166.0 1.3 collective-permute-start.5
  167.3 6.6 %collective-permute-done.10 = f32[16,8320]{1,0:T(8,128)S(1)} collective-permute-done((f32[16,8320]{1,0:T(8,128)S(1)}, f32[16,8320]{1,0:T(8,128)S(1)}, u32[]{:S(2)}, u32[]{:S(2)}) %collective-permute-start.10) | collective-permute-done | bytes 532512 | tf_op jit(solution)/shard_map/ppermute | solution.py:14
  174.1 8.2 %collective-permute-start.11 = (f32[16,8320]{1,0:T(8,128)S(1)}, f32[16,8320]{1,0:T(8,128)}, u32[]{:S(2)}, u32[]{:S(2)}) collective-permute-start(f32[16,8320]{1,0:T(8,128)S(1)} %pad_maximum_fusion.9), channel_id=1, source_target_pairs={{0,16},{1,17},{2,18},{3,19},{4,20},{5,21},{6,22},{7,23},{8,24},{9,... | collective-permute-start | bytes 1597448 | tf_op jit(solution)/shard_map/ppermute | solution.py:14
  182.4 0.7 slice_reduce_fusion.1
  183.1 2.5 collective-permute-done.5
  185.6 0.2 fusion.18
  185.7 0.5 convert_element_type.100
  186.3 0.2 copy.54
  186.5 0.9 convolution_bitcast_fusion.7
  187.4 0.2 fusion.37
  187.6 0.6 collective-permute-done.11
  188.3 1.2 fusion.13
  189.4 0.5 convert_element_type.111
  190.0 1.0 fusion.6
  191.0 0.3 convolution_bitcast_fusion.6
  191.4 1.4 fusion.5
  192.9 5.3 %convolution_bitcast_fusion = f32[2048,1280]{0,1:T(8,128)} fusion(bf16[1,128,2048]{2,1,0:T(8,128)(2,1)S(1)} %copy-done, bf16[128,128]{0,1:T(8,128)(2,1)S(1)} %fusion.7, bf16[128,128]{0,1:T(8,128)(2,1)S(1)} %fusion.6, bf16[128,1024]{0,1:T(8,128)(2,1)S(1)} %bitcast.106), kind=kOutput, calls=%fused_computation | convolution fusion | flops 672071680 | bytes 11337728 | tf_op jit(solution)/shard_map/dot_general | solution.py:164
  198.2 11.3 %copy.72 = f32[2048,1280]{1,0:T(8,128)} copy(f32[2048,1280]{0,1:T(8,128)} %convolution_bitcast_fusion) | data formatting | bytes 20971520
  209.6 113.2 %reduce-scatter.4.cloned.1.call-done = f32[64,1280]{1,0:T(8,128)} async-done(((f32[2048,1280]{1,0:T(8,128)}), f32[64,1280]{1,0:T(8,128)}) %reduce-scatter.4.cloned.1.call-update) | async-done | bytes 327696
  322.8 2.0 copy.73
  324.9 5.3 %convolution_bitcast_fusion.1 = f32[1,128,2048]{2,1,0:T(8,128)} fusion(bf16[2048,1280]{1,0:T(8,128)(2,1)} %bitcast, bf16[128,128]{0,1:T(8,128)(2,1)S(1)} %fusion.7, bf16[128,128]{0,1:T(8,128)(2,1)S(1)} %fusion.6, bf16[128,1024]{0,1:T(8,128)(2,1)S(1)} %bitcast.107), kind=kOutput, calls=%fused_computation.1 | convolution fusion | flops 672071680 | bytes 6619136 | tf_op jit(solution)/shard_map/dot_general | solution.py:157
  330.2 68.8 %all-reduce.2.cloned.1.call-done = f32[64,1280]{0,1:T(8,128)} async-done(((f32[64,1280]{0,1:T(8,128)}), f32[64,1280]{0,1:T(8,128)}) %all-reduce.2.cloned.1.call-update) | async-done | bytes 327696 | tf_op jit(solution)/shard_map/psum | solution.py:171
  399.0 1.1 broadcast_multiply_fusion
  400.1 0.9 copy.62
  (59 shorter events, 3.0 us)
Async XLA Ops:
  7.2 76.0 %copy-start = (bf16[1,128,2048]{2,1,0:T(8,128)(2,1)S(1)}, bf16[1,128,2048]{2,1,0:T(8,128)(2,1)}, u32[]{:S(2)}) copy-start(bf16[1,128,2048]{2,1,0:T(8,128)(2,1)} %param.5) | copy-start | bytes 1572868
  12.1 7.9 %copy-start.3 = (f32[1,16,128]{2,1,0:T(8,128)S(1)}, f32[1,16,128]{2,1,0:T(8,128)}, u32[]{:S(2)}) copy-start(f32[1,16,128]{2,1,0:T(8,128)} %param.8) | copy-start | bytes 24580
  12.1 8.4 %copy-start.2 = (bf16[1,128,1024]{2,1,0:T(8,128)(2,1)S(1)}, bf16[1,128,1024]{2,1,0:T(8,128)(2,1)}, u32[]{:S(2)}) copy-start(bf16[1,128,1024]{2,1,0:T(8,128)(2,1)} %param.9) | copy-start | bytes 786436
  12.1 71.0 %all-to-all-start = ((bf16[32,64,1280]{2,1,0:T(8,128)(2,1)}), bf16[32,64,1280]{2,1,0:T(8,128)(2,1)}, u32[]{:S(2)}, u32[]{:S(2)}) async-start(bf16[32,64,1280]{2,1,0:T(8,128)(2,1)} %stack.2), calls=%async_computation | async-start | bytes 10485760 | tf_op jit(solution)/shard_map/all_to_all | solution.py:119
  20.0 302.8 %reduce-scatter.4.cloned.1.call-start = ((), (), s32[]{:S(2)}) async-start(), calls=%async_computation.3 | async-start | bytes 10813440
  21.8 66.4 %copy-start.4 = (f32[128,16]{0,1:T(8,128)}, f32[128,16]{0,1:T(8,128)S(1)}, u32[]{:S(2)}) copy-start(f32[128,16]{0,1:T(8,128)S(1)} %get-tuple-element.80) | copy-start | bytes 24580
  90.1 8.7 %collective-permute-start = (f32[16,8320]{1,0:T(8,128)S(1)}, f32[16,8320]{1,0:T(8,128)S(1)}, u32[]{:S(2)}, u32[]{:S(2)}) collective-permute-start(f32[16,8320]{1,0:T(8,128)S(1)} %get-tuple-element.94), channel_id=1, source_target_pairs={{1,0},{2,1},{3,2},{4,3},{5,4},{6,5},{7,6},{8,7},{9,8},{10,9},{11,1... | collective-permute-start | bytes 1597448 | tf_op jit(solution)/shard_map/ppermute | solution.py:14
  92.0 12.4 %collective-permute-start.6 = (f32[16,8320]{1,0:T(8,128)S(1)}, f32[16,8320]{1,0:T(8,128)S(1)}, u32[]{:S(2)}, u32[]{:S(2)}) collective-permute-start(f32[16,8320]{1,0:T(8,128)S(1)} %get-tuple-element.95), channel_id=1, source_target_pairs={{0,1},{1,2},{2,3},{3,4},{4,5},{5,6},{6,7},{7,8},{8,9},{9,10},{10,1... | collective-permute-start | bytes 1597448 | tf_op jit(solution)/shard_map/ppermute | solution.py:14
  94.5 30.7 %copy-start.5 = (pred[128,128]{0,1:T(8,128)(4,1)}, pred[128,128]{0,1:T(8,128)(4,1)S(1)}, u32[]{:S(2)}) copy-start(pred[128,128]{0,1:T(8,128)(4,1)S(1)} %iota_compare_fusion) | copy-start | bytes 49156
  98.8 10.6 %collective-permute-start.1 = (f32[16,8320]{1,0:T(8,128)S(1)}, f32[16,8320]{1,0:T(8,128)S(1)}, u32[]{:S(2)}, u32[]{:S(2)}) collective-permute-start(f32[16,8320]{1,0:T(8,128)S(1)} %collective-permute-done), channel_id=1, source_target_pairs={{1,0},{2,1},{3,2},{4,3},{5,4},{6,5},{7,6},{8,7},{9,8},{10,9},{11,1... | collective-permute-start | bytes 1597448 | tf_op jit(solution)/shard_map/ppermute | solution.py:14
  104.4 10.6 %collective-permute-start.7 = (f32[16,8320]{1,0:T(8,128)S(1)}, f32[16,8320]{1,0:T(8,128)S(1)}, u32[]{:S(2)}, u32[]{:S(2)}) collective-permute-start(f32[16,8320]{1,0:T(8,128)S(1)} %collective-permute-done.6), channel_id=1, source_target_pairs={{0,1},{1,2},{2,3},{3,4},{4,5},{5,6},{6,7},{7,8},{8,9},{9,10},{10,1... | collective-permute-start | bytes 1597448 | tf_op jit(solution)/shard_map/ppermute | solution.py:14
  109.6 15.4 %collective-permute-start.2 = (f32[16,8320]{1,0:T(8,128)S(1)}, f32[16,8320]{1,0:T(8,128)S(1)}, u32[]{:S(2)}, u32[]{:S(2)}) collective-permute-start(f32[16,8320]{1,0:T(8,128)S(1)} %pad_maximum_fusion.2), channel_id=1, source_target_pairs={{2,0},{3,1},{4,2},{5,3},{6,4},{7,5},{8,6},{9,7},{10,8},{11,9},{12,... | collective-permute-start | bytes 1597448 | tf_op jit(solution)/shard_map/ppermute | solution.py:14
  115.2 15.3 %collective-permute-start.8 = (f32[16,8320]{1,0:T(8,128)S(1)}, f32[16,8320]{1,0:T(8,128)S(1)}, u32[]{:S(2)}, u32[]{:S(2)}) collective-permute-start(f32[16,8320]{1,0:T(8,128)S(1)} %pad_maximum_fusion.6), channel_id=1, source_target_pairs={{0,2},{1,3},{2,4},{3,5},{4,6},{5,7},{6,8},{7,9},{8,10},{9,11},{10,... | collective-permute-start | bytes 1597448 | tf_op jit(solution)/shard_map/ppermute | solution.py:14
  125.2 26.5 %collective-permute-start.3 = (f32[16,8320]{1,0:T(8,128)S(1)}, f32[16,8320]{1,0:T(8,128)S(1)}, u32[]{:S(2)}, u32[]{:S(2)}) collective-permute-start(f32[16,8320]{1,0:T(8,128)S(1)} %pad_maximum_fusion.3), channel_id=1, source_target_pairs={{4,0},{5,1},{6,2},{7,3},{8,4},{9,5},{10,6},{11,7},{12,8},{13,9},{1... | collective-permute-start | bytes 1597448 | tf_op jit(solution)/shard_map/ppermute | solution.py:14
  130.6 29.9 %collective-permute-start.9 = (f32[16,8320]{1,0:T(8,128)S(1)}, f32[16,8320]{1,0:T(8,128)S(1)}, u32[]{:S(2)}, u32[]{:S(2)}) collective-permute-start(f32[16,8320]{1,0:T(8,128)S(1)} %pad_maximum_fusion.7), channel_id=1, source_target_pairs={{0,4},{1,5},{2,6},{3,7},{4,8},{5,9},{6,10},{7,11},{8,12},{9,13},{1... | collective-permute-start | bytes 1597448 | tf_op jit(solution)/shard_map/ppermute | solution.py:14
  151.9 13.9 %collective-permute-start.4 = (f32[16,8320]{1,0:T(8,128)S(1)}, f32[16,8320]{1,0:T(8,128)S(1)}, u32[]{:S(2)}, u32[]{:S(2)}) collective-permute-start(f32[16,8320]{1,0:T(8,128)S(1)} %pad_maximum_fusion.4), channel_id=1, source_target_pairs={{8,0},{9,1},{10,2},{11,3},{12,4},{13,5},{14,6},{15,7},{16,8},{17,9... | collective-permute-start | bytes 1597448 | tf_op jit(solution)/shard_map/ppermute | solution.py:14
  160.5 26.0 %copy-start.1 = (bf16[128,1024]{0,1:T(8,128)(2,1)S(1)}, bf16[128,1024]{0,1:T(8,128)(2,1)}, u32[]{:S(2)}) copy-start(bf16[128,1024]{0,1:T(8,128)(2,1)} %get-tuple-element.75) | copy-start | bytes 786436
  160.7 13.2 %collective-permute-start.10 = (f32[16,8320]{1,0:T(8,128)S(1)}, f32[16,8320]{1,0:T(8,128)S(1)}, u32[]{:S(2)}, u32[]{:S(2)}) collective-permute-start(f32[16,8320]{1,0:T(8,128)S(1)} %pad_maximum_fusion.8), channel_id=1, source_target_pairs={{0,8},{1,9},{2,10},{3,11},{4,12},{5,13},{6,14},{7,15},{8,16},{9,17... | collective-permute-start | bytes 1597448 | tf_op jit(solution)/shard_map/ppermute | solution.py:14
  166.0 19.6 %collective-permute-start.5 = (f32[16,8320]{1,0:T(8,128)S(1)}, f32[16,8320]{1,0:T(8,128)S(1)}, u32[]{:S(2)}, u32[]{:S(2)}) collective-permute-start(f32[16,8320]{1,0:T(8,128)S(1)} %pad_maximum_fusion.5), channel_id=1, source_target_pairs={{16,0},{17,1},{18,2},{19,3},{20,4},{21,5},{22,6},{23,7},{24,8},{25... | collective-permute-start | bytes 1597448 | tf_op jit(solution)/shard_map/ppermute | solution.py:14
  174.1 14.2 %collective-permute-start.11 = (f32[16,8320]{1,0:T(8,128)S(1)}, f32[16,8320]{1,0:T(8,128)}, u32[]{:S(2)}, u32[]{:S(2)}) collective-permute-start(f32[16,8320]{1,0:T(8,128)S(1)} %pad_maximum_fusion.9), channel_id=1, source_target_pairs={{0,16},{1,17},{2,18},{3,19},{4,20},{5,21},{6,22},{7,23},{8,24},{9,... | collective-permute-start | bytes 1597448 | tf_op jit(solution)/shard_map/ppermute | solution.py:14
  209.5 189.4 %all-reduce.2.cloned.1.call-start = ((), (), s32[]{:S(2)}) async-start(), calls=%async_computation.2 | async-start | bytes 1310720 | tf_op jit(solution)/shard_map/psum | solution.py:171
Sparse Core Ops, SparseCore 0:
  209.7 113.0 reduce-scatter.3
  325.2 73.6 all-reduce.1
